TPU v7x, 32 devices: a whole 2x2x4 slice. The times are simulated.
32 devices in a mesh: member: 2 (over y), lon: 4 (over z), lev: 4 (over x, core).
Axes of the slice: x: 2, y: 2, z: 4, core: 2. Of those that a mesh axis runs over, the one named last changes fastest.
Arguments:
- latent: bfloat16 [512, 8, 512], P('lev', 'member', 'lon'), parts along dimension 1, may hold values from -9 to 9
- att_gain: float32 [512], replicated, may hold values from 0.1 to 1.9
- qkv_weight: bfloat16 [3, 512, 512], P(None, 'lev'), may hold values from -0.25 to 0.25
- out_weight: bfloat16 [512, 512], P('lev'), may hold values from -0.25 to 0.25
- stencil_weight: float32 [2, 9, 512], P(None, None, 'lev'), may hold values from -2.5 to 2.5
- block_gain: float32 [2, 512], replicated, may hold values from 0.1 to 1.9
- up_weight: bfloat16 [2, 2048, 512], P(None, 'lev'), may hold values from -0.25 to 0.25
- down_weight: bfloat16 [2, 2048, 512], P(None, 'lev'), may hold values from -0.125 to 0.125
Outputs:
- decoded: bfloat16 [512, 8, 512], P('lev', 'member', 'lon'), parts along dimension 1
There are 2 independent parts, one for each index of `member`. A program takes and returns all parts, laid end to end along the dimension named above; an argument that names none is the same for every part. Nothing has to cross between parts.
All inputs are finite; a program needn't handle non-finite values.
Results may differ from a plain program's by a relative error of at most 0.017.
Values may be sent and summed in bfloat16 or wider, within the bound.
No kernel may reach another device: no remote copies, remote signals or barrier semaphores. Data moves between devices by JAX's collectives and lax.ppermute only.
A program may use at most 64 MiB of HBM per device.

v0:
```python
import math
import jax
import jax.numpy as jnp
from jax import lax
from jax.sharding import PartitionSpec as P

C = 512
H = 8
BLOCKS = 2
attention_scale = 24.0
band_start = 30.0
grid_step = 0.25
epsilon = 1e-06


def secant_rows(count):
    rows = jnp.arange(count).astype(jnp.float32)
    return 1.0 / jnp.cos((band_start + grid_step * rows) * (math.pi / 180.0))


def norm_channels(values, gain):
    scale = lax.rsqrt(jnp.mean(values * values, axis=0, keepdims=True) + epsilon)
    return values * scale * gain[:, None, None]


def unit_heads(values):
    return values * lax.rsqrt(jnp.sum(values * values, axis=1, keepdims=True) + epsilon)


def gather_channels(values):
    return lax.all_gather(values, "lev", axis=0, tiled=True)


def scatter_sum(partial, axis, halo=False):
    devices = lax.axis_size(axis)
    me = lax.axis_index(axis)
    strips = lax.axis_size("lon")
    blocks = partial.reshape(devices, -1, *partial.shape[1:])
    total = jnp.take(blocks, me, axis=0).astype(jnp.float32)
    before = jnp.zeros(total.shape[:-1] + (1,), jnp.float32)
    after = jnp.zeros(total.shape[:-1] + (1,), jnp.float32)
    for shift in range(devices):
        chunk = jnp.take(blocks, (me + shift) % devices, axis=0)
        if shift:
            pairs = [(i, (i + shift) % devices) for i in range(devices)]
            total = total + lax.ppermute(chunk, axis, pairs).astype(jnp.float32)
        if halo:
            for step, edge, sums in ((1, chunk[..., -1:], "before"), (-1, chunk[..., :1], "after")):
                pairs = [
                    (s * devices + i, (s + step) % strips * devices + (i + shift) % devices)
                    for s in range(strips)
                    for i in range(devices)
                ]
                got = lax.ppermute(edge, ("lon", axis), pairs).astype(jnp.float32)
                if sums == "before":
                    before = before + got
                else:
                    after = after + got
    return (total, before, after)


def spread_sum(weight, activation, shape, halo=False):
    partial = lax.dot_general(
        weight, activation, (((0,), (0,)), ((), ())), preferred_element_type=jnp.float32
    ).astype(jnp.bfloat16)
    return scatter_sum(partial.reshape(weight.shape[1], *shape), "lev", halo)


def add_update(state, sums):
    return tuple(((s.astype(jnp.float32) + u).astype(jnp.bfloat16) for s, u in zip(state, sums)))


def gather_strips(values, axis):
    devices = lax.axis_size(axis)
    pieces = [values]
    for shift in range(1, devices):
        pairs = [(i, (i + shift) % devices) for i in range(devices)]
        pieces.append(lax.ppermute(values, axis, pairs))
    return jnp.concatenate(pieces, axis=-1)


def make_fold(queries, pieces):
    key_part, value_part = pieces
    scores = (
        jnp.einsum("hdri,hdrj->hrij", queries, key_part, preferred_element_type=jnp.float32)
        * attention_scale
    )
    weights = jnp.exp(scores)
    numerator = jnp.einsum(
        "hrij,hdrj->hdri",
        weights.astype(jnp.bfloat16),
        value_part,
        preferred_element_type=jnp.float32,
    )
    return (numerator, jnp.sum(weights, axis=3))


def block_apply(state, block_index, stencil_weight, block_gain, up_weight, down_weight, halo):
    extended = jnp.concatenate([state[1], state[0], state[2]], axis=2)
    lat_rows = extended.shape[1]
    out_cols = extended.shape[2] - 2
    secants = secant_rows(lat_rows)[None, :, None]
    padded = jnp.pad(extended.astype(jnp.float32), ((0, 0), (1, 1), (0, 0)))
    tap_weights = stencil_weight[block_index]
    stencil_sum = jnp.zeros((extended.shape[0], lat_rows, out_cols), jnp.float32)
    for row_step in (-1, 0, 1):
        for col_step in (-1, 0, 1):
            shifted = padded[
                :, 1 + row_step : 1 + row_step + lat_rows, 1 + col_step : 1 + col_step + out_cols
            ]
            tap_row = tap_weights[3 * (row_step + 1) + col_step + 1][:, None, None]
            if col_step != 0:
                stencil_sum = stencil_sum + tap_row * secants * shifted
            else:
                stencil_sum = stencil_sum + tap_row * shifted
    smoothed = stencil_sum.astype(jnp.bfloat16)
    full_channels = gather_channels(smoothed)
    block_normed = norm_channels(full_channels.astype(jnp.float32), block_gain[block_index]).astype(
        jnp.bfloat16
    )
    block_normed = block_normed.reshape(full_channels.shape[0], -1)
    hidden = jax.nn.gelu(
        jnp.dot(up_weight[block_index], block_normed, preferred_element_type=jnp.float32)
    ).astype(jnp.bfloat16)
    sums = spread_sum(down_weight[block_index], hidden, state[0].shape[1:], halo)
    return add_update(state, sums)


def per_device(
    latent, att_gain, qkv_weight, out_weight, stencil_weight, block_gain, up_weight, down_weight
):
    ch_local, lat_rows, columns = latent.shape
    head_size = C // H
    heads_local = qkv_weight.shape[1] // head_size
    gathered = gather_channels(latent)
    normed = norm_channels(gathered.astype(jnp.float32), att_gain).astype(jnp.bfloat16)
    projected = jnp.einsum("koc,crw->korw", qkv_weight, normed, preferred_element_type=jnp.float32)
    projected = projected.reshape(3, heads_local, head_size, lat_rows, columns)
    queries = unit_heads(projected[0]).astype(jnp.bfloat16)
    key_rows = unit_heads(projected[1]).astype(jnp.bfloat16)
    value_rows = projected[2].astype(jnp.bfloat16)
    key_value = gather_strips(jnp.stack([key_rows, value_rows]), "lon")
    numerator, denominator = make_fold(queries, (key_value[0], key_value[1]))
    attended = (numerator / denominator[:, None]).astype(jnp.bfloat16)
    strips = lax.axis_size("lon")
    latent_before = lax.ppermute(
        latent[..., -1:], "lon", [(i, (i + 1) % strips) for i in range(strips)]
    )
    latent_after = lax.ppermute(
        latent[..., :1], "lon", [(i, (i - 1) % strips) for i in range(strips)]
    )
    sums = spread_sum(out_weight, attended.reshape(ch_local, -1), latent.shape[1:], True)
    current = add_update((latent, latent_before, latent_after), sums)
    for block_index in range(BLOCKS):
        current = block_apply(
            current,
            block_index,
            stencil_weight,
            block_gain,
            up_weight,
            down_weight,
            block_index < BLOCKS - 1,
        )
    return current[0]


def solution(mesh):
    placed = (
        P("lev", "member", "lon"),
        P(),
        P(None, "lev", None),
        P("lev", None),
        P(None, None, "lev"),
        P(),
        P(None, "lev", None),
        P(None, "lev", None),
    )
    return jax.shard_map(
        per_device, mesh=mesh, in_specs=placed, out_specs=P("lev", "member", "lon"), check_vma=False
    )
```

profile of v0, /device:TPU:0, one launch (start us, length us, event | category | flops | bytes accessed | tf_op | source)
XLA Modules:
  0.0 121.0 jit_solution(17095749814816326519)
XLA Ops:
  0.0 8.9 %all_gather.9 = bf16[512,4,128]{2,1,0:T(4,128)(2,1)S(1)} all-gather(bf16[128,4,128]{2,1,0:T(4,128)(2,1)} %param.10), channel_id=1, replica_groups=mesh['member'=2,'lon'=4,'lev'=4] {'lev'}, dimensions={0}, use_global_device_ids=true | all-gather | bytes 655360 | tf_op jit(solution)/shard_map/all_gather | solution.py:31
  9.5 1.9 %fusion.34 = bf16[512,4,128,1]{2,1,0,3:T(4,128)(2,1)S(1)} fusion(bf16[512,4,128]{2,1,0:T(4,128)(2,1)S(1)} %all_gather.9, f32[512]{0:T(512)} %param.11, f32[4,128]{1,0:T(4,128)S(1)} %add_rsqrt_fusion.4), kind=kLoop, calls=%fused_computation.62 | loop fusion | flops 1048576 | bytes 1052672 | tf_op jit(solution)/shard_map/convert_element_type | solution.py:136
  12.1 3.7 %collective-permute-start.2 = (bf16[2,2,64,4,128]{4,2,3,1,0:T(8,128)(2,1)S(1)}, bf16[2,2,64,4,128]{4,2,3,1,0:T(8,128)(2,1)S(1)}, u32[]{:S(2)}, u32[]{:S(2)}) collective-permute-start(bf16[2,2,64,4,128]{4,2,3,1,0:T(8,128)(2,1)S(1)} %pad_maximum_fusion.1), channel_id=1, source_target_pairs={{0,12},{4,0},{8,4},{12,8},{1,13},{5,1},{9,5},{13,9},{2,14},{6,2},{... | collective-permute-start | bytes 786440 | tf_op jit(solution)/shard_map/ppermute | solution.py:78
  16.9 2.9 %collective-permute-start.11 = (bf16[128,4,1]{0,1,2:T(4,128)(2,1)S(1)}, bf16[128,4,1]{0,1,2:T(4,128)(2,1)S(1)}, u32[]{:S(2)}, u32[]{:S(2)}) collective-permute-start(bf16[128,4,1]{0,1,2:T(4,128)(2,1)S(1)} %get-tuple-element.43), channel_id=1, source_target_pairs={{0,12},{4,0},{8,4},{12,8},{1,13},{5,1},{9,5},{13,9},{2,14},{6,2},{... | collective-permute-start | bytes 3080 | tf_op jit(solution)/shard_map/ppermute | solution.py:149
  20.1 2.4 %collective-permute-done.2 = bf16[2,2,64,4,128]{4,2,3,1,0:T(8,128)(2,1)S(1)} collective-permute-done((bf16[2,2,64,4,128]{4,2,3,1,0:T(8,128)(2,1)S(1)}, bf16[2,2,64,4,128]{4,2,3,1,0:T(8,128)(2,1)S(1)}, u32[]{:S(2)}, u32[]{:S(2)}) %collective-permute-start.2) | collective-permute-done | bytes 262176 | tf_op jit(solution)/shard_map/ppermute | solution.py:78
  22.5 16.1 %collective-permute-done.1 = bf16[2,2,64,4,128]{4,2,3,1,0:T(8,128)(2,1)S(1)} collective-permute-done((bf16[2,2,64,4,128]{4,2,3,1,0:T(8,128)(2,1)S(1)}, bf16[2,2,64,4,128]{4,2,3,1,0:T(8,128)(2,1)S(1)}, u32[]{:S(2)}, u32[]{:S(2)}) %collective-permute-start.1) | collective-permute-done | bytes 262176 | tf_op jit(solution)/shard_map/ppermute | solution.py:78
  40.7 1.4 %constant_dynamic-slice_fusion.12 = (bf16[1,128,4,128]{1,0,3,2:T(2,128)(2,1)S(1)}, bf16[1,128,4,128]{1,0,3,2:T(2,128)(2,1)S(1)}, bf16[1,128,4,128]{1,0,3,2:T(2,1...) fusion(bf16[4,128,4,128]{1,0,3,2:T(4,128)(2,1)S(1)} %reshape.765, s32[]{:T(128)S(6)} %select_n.83, ...), kind=kLoop, calls=%fused_computation.180 | loop fusion | bytes 1310740 | tf_op jit(solution)/shard_map/jit(_take) | solution.py:39
  42.6 4.1 %collective-permute-start.14 = (bf16[128,4,1]{0,1,2:T(4,128)(2,1)S(1)}, bf16[128,4,1]{0,1,2:T(4,128)(2,1)S(1)}, u32[]{:S(2)}, u32[]{:S(2)}) collective-permute-start(bf16[128,4,1]{0,1,2:T(4,128)(2,1)S(1)} %get-tuple-element.49), channel_id=1, source_target_pairs={{0,14},{1,15},{2,12},{3,13},{4,2},{5,3},{6,0},{7,1},{8,6},{9,7},{1... | collective-permute-start | bytes 3080 | tf_op jit(solution)/shard_map/ppermute | solution.py:54
  48.1 1.4 %collective-permute-start.6 = (bf16[128,4,1]{0,1,2:T(4,128)(2,1)S(1)}, bf16[128,4,1]{0,1,2:T(4,128)(2,1)S(1)}, u32[]{:S(2)}, u32[]{:S(2)}) collective-permute-start(bf16[128,4,1]{0,1,2:T(4,128)(2,1)S(1)} %get-tuple-element.42), channel_id=1, source_target_pairs={{0,4},{4,8},{8,12},{12,0},{1,5},{5,9},{9,13},{13,1},{2,6},{6,10},{... | collective-permute-start | bytes 3080 | tf_op jit(solution)/shard_map/ppermute | solution.py:146
  49.5 1.9 %collective-permute-start.10 = (bf16[128,4,1]{0,1,2:T(4,128)(2,1)S(1)}, bf16[128,4,1]{0,1,2:T(4,128)(2,1)S(1)}, u32[]{:S(2)}, u32[]{:S(2)}) collective-permute-start(bf16[128,4,1]{0,1,2:T(4,128)(2,1)S(1)} %get-tuple-element.50), channel_id=1, source_target_pairs={{0,7},{1,4},{2,5},{3,6},{4,11},{5,8},{6,9},{7,10},{8,15},{9,12},{1... | collective-permute-start | bytes 3080 | tf_op jit(solution)/shard_map/ppermute | solution.py:54
  52.9 1.4 %collective-permute-start.7 = (bf16[128,4,1]{0,1,2:T(4,128)(2,1)S(1)}, bf16[128,4,1]{0,1,2:T(4,128)(2,1)S(1)}, u32[]{:S(2)}, u32[]{:S(2)}) collective-permute-start(bf16[128,4,1]{0,1,2:T(4,128)(2,1)S(1)} %get-tuple-element.44), channel_id=1, source_target_pairs={{0,4},{1,5},{2,6},{3,7},{4,8},{5,9},{6,10},{7,11},{8,12},{9,13},{1... | collective-permute-start | bytes 3080 | tf_op jit(solution)/shard_map/ppermute | solution.py:54
  54.3 2.1 %collective-permute-start.5 = (bf16[128,4,128]{0,1,2:T(4,128)(2,1)S(1)}, bf16[128,4,128]{0,1,2:T(4,128)(2,1)S(1)}, u32[]{:S(2)}, u32[]{:S(2)}) collective-permute-start(bf16[128,4,128]{0,1,2:T(4,128)(2,1)S(1)} %fusion.109), channel_id=1, source_target_pairs={{0,3},{1,0},{2,1},{3,2},{4,7},{5,4},{6,5},{7,6},{8,11},{9,8},{10,9... | collective-permute-start | bytes 393224 | tf_op jit(solution)/shard_map/ppermute | solution.py:46
  58.3 1.9 %collective-permute-done.5 = bf16[128,4,128]{0,1,2:T(4,128)(2,1)S(1)} collective-permute-done((bf16[128,4,128]{0,1,2:T(4,128)(2,1)S(1)}, bf16[128,4,128]{0,1,2:T(4,128)(2,1)S(1)}, u32[]{:S(2)}, u32[]{:S(2)}) %collective-permute-start.5) | collective-permute-done | bytes 131104 | tf_op jit(solution)/shard_map/ppermute | solution.py:46
  60.2 4.0 %collective-permute-done.4 = bf16[128,4,128]{0,1,2:T(4,128)(2,1)S(1)} collective-permute-done((bf16[128,4,128]{0,1,2:T(4,128)(2,1)S(1)}, bf16[128,4,128]{0,1,2:T(4,128)(2,1)S(1)}, u32[]{:S(2)}, u32[]{:S(2)}) %collective-permute-start.4) | collective-permute-done | bytes 131104 | tf_op jit(solution)/shard_map/ppermute | solution.py:46
  65.2 6.8 %all_gather.10 = bf16[512,4,128]{2,1,0:T(4,128)(2,1)S(1)} all-gather(bf16[128,4,128]{2,1,0:T(4,128)(2,1)S(1)} %copy.93), channel_id=1, replica_groups=mesh['member'=2,'lon'=4,'lev'=4] {'lev'}, dimensions={0}, use_global_device_ids=true | all-gather | bytes 655360 | tf_op jit(solution)/shard_map/all_gather | solution.py:31
  72.5 1.5 %fusion.12 = bf16[512,4,128]{2,1,0:T(4,128)(2,1)S(1)} fusion(bf16[512,4,128]{2,1,0:T(4,128)(2,1)S(1)} %all_gather.10, f32[512]{0:T(512)S(1)} %bitcast.161, f32[4,128]{1,0:T(4,128)S(1)} %add_rsqrt_fusion.3), kind=kLoop, calls=%fused_computation.28 | loop fusion | flops 1048576 | bytes 1052672 | tf_op jit(solution)/shard_map/convert_element_type | solution.py:118
  74.0 2.0 %fusion.3 = bf16[512,512]{0,1:T(8,128)(2,1)S(1)} fusion(bf16[64,8,4,128]{3,2,1,0:T(4,128)(2,1)S(1)} %bitcast.157, bf16[2,512,512]{2,1,0:T(8,128)(2,1)S(1)} %copy-done.5, bf16[2,512,512]{2,1,0:T(8,128)(2,1)} %param.16), kind=kOutput, calls=%fused_computation.18 | convolution fusion | flops 539492352 | bytes 2097152 | tf_op jit(solution)/shard_map/dot_general | solution.py:63
  76.2 1.5 %constant_dynamic-slice_fusion.5 = (bf16[1,128,4,128]{1,0,3,2:T(2,128)(2,1)S(1)}, bf16[1,128,4,128]{1,0,3,2:T(2,128)(2,1)S(1)}, bf16[1,128,4,128]{1,0,3,2:T(2,12...) fusion(bf16[4,128,4,128]{1,0,3,2:T(4,128)(2,1)S(1)} %reshape.766, s32[]{:T(128)S(6)} %select_n.83, ...), kind=kLoop, calls=%fused_computation.173 | loop fusion | bytes 1310740 | tf_op jit(solution)/shard_map/jit(_take) | solution.py:39
  77.9 2.7 %collective-permute-start.26 = (bf16[128,4,1]{0,1,2:T(4,128)(2,1)S(1)}, bf16[128,4,1]{0,1,2:T(4,128)(2,1)S(1)}, u32[]{:S(2)}, u32[]{:S(2)}) collective-permute-start(bf16[128,4,1]{0,1,2:T(4,128)(2,1)S(1)} %get-tuple-element.41), channel_id=1, source_target_pairs={{0,15},{1,12},{2,13},{3,14},{4,3},{5,0},{6,1},{7,2},{8,7},{9,4},{1... | collective-permute-start | bytes 3080 | tf_op jit(solution)/shard_map/ppermute | solution.py:54
  82.9 1.1 collective-permute-start.23
  84.0 1.5 %collective-permute-start.18 = (bf16[128,4,128]{0,1,2:T(4,128)(2,1)S(1)}, bf16[128,4,128]{0,1,2:T(4,128)(2,1)S(1)}, u32[]{:S(2)}, u32[]{:S(2)}) collective-permute-start(bf16[128,4,128]{0,1,2:T(4,128)(2,1)S(1)} %fusion.104), channel_id=1, source_target_pairs={{0,3},{1,0},{2,1},{3,2},{4,7},{5,4},{6,5},{7,6},{8,11},{9,8},{10,9... | collective-permute-start | bytes 393224 | tf_op jit(solution)/shard_map/ppermute | solution.py:46
  87.3 1.3 %collective-permute-start.20 = (bf16[128,4,1]{0,1,2:T(4,128)(2,1)S(1)}, bf16[128,4,1]{0,1,2:T(4,128)(2,1)S(1)}, u32[]{:S(2)}, u32[]{:S(2)}) collective-permute-start(bf16[128,4,1]{0,1,2:T(4,128)(2,1)S(1)} %get-tuple-element.36), channel_id=1, source_target_pairs={{0,5},{1,6},{2,7},{3,4},{4,9},{5,10},{6,11},{7,8},{8,13},{9,14},{1... | collective-permute-start | bytes 3080 | tf_op jit(solution)/shard_map/ppermute | solution.py:54
  88.7 1.7 %collective-permute-start.19 = (bf16[128,4,1]{0,1,2:T(4,128)(2,1)S(1)}, bf16[128,4,1]{0,1,2:T(4,128)(2,1)S(1)}, u32[]{:S(2)}, u32[]{:S(2)}) collective-permute-start(bf16[128,4,1]{0,1,2:T(4,128)(2,1)S(1)} %get-tuple-element.34), channel_id=1, source_target_pairs={{0,4},{1,5},{2,6},{3,7},{4,8},{5,9},{6,10},{7,11},{8,12},{9,13},{1... | collective-permute-start | bytes 3080 | tf_op jit(solution)/shard_map/ppermute | solution.py:54
  91.4 1.2 collective-permute-done.21
  94.1 2.4 %collective-permute-done.17 = bf16[128,4,128]{0,1,2:T(4,128)(2,1)S(1)} collective-permute-done((bf16[128,4,128]{0,1,2:T(4,128)(2,1)S(1)}, bf16[128,4,128]{0,1,2:T(4,128)(2,1)S(1)}, u32[]{:S(2)}, u32[]{:S(2)}) %collective-permute-start.17) | collective-permute-done | bytes 131104 | tf_op jit(solution)/shard_map/ppermute | solution.py:46
  98.4 6.8 %all_gather.11 = bf16[512,4,128]{2,1,0:T(4,128)(2,1)S(1)} all-gather(bf16[128,4,128]{2,1,0:T(4,128)(2,1)S(1)} %copy.100), channel_id=1, replica_groups=mesh['member'=2,'lon'=4,'lev'=4] {'lev'}, dimensions={0}, use_global_device_ids=true | all-gather | bytes 655360 | tf_op jit(solution)/shard_map/all_gather | solution.py:31
  105.8 1.5 %fusion.15 = bf16[512,4,128]{2,1,0:T(4,128)(2,1)S(1)} fusion(bf16[512,4,128]{2,1,0:T(4,128)(2,1)S(1)} %all_gather.11, f32[512]{0:T(512)S(1)} %bitcast.160, f32[4,128]{1,0:T(4,128)S(1)} %add_rsqrt_fusion.2), kind=kLoop, calls=%fused_computation.31 | loop fusion | flops 1048576 | bytes 1052672 | tf_op jit(solution)/shard_map/convert_element_type | solution.py:118
  107.3 2.0 %fusion.4 = bf16[512,512]{0,1:T(8,128)(2,1)S(1)} fusion(bf16[64,8,4,128]{3,2,1,0:T(4,128)(2,1)S(1)} %bitcast.158, bf16[2,512,512]{2,1,0:T(8,128)(2,1)S(1)} %copy-done.5, bf16[2,512,512]{2,1,0:T(8,128)(2,1)} %param.16), kind=kOutput, calls=%fused_computation.19 | convolution fusion | flops 539492352 | bytes 2097152 | tf_op jit(solution)/shard_map/dot_general | solution.py:63
  109.4 1.2 %constant_dynamic-slice_fusion.13 = (bf16[1,128,4,128]{1,0,3,2:T(2,128)(2,1)S(1)}, bf16[1,128,4,128]{1,0,3,2:T(2,128)(2,1)S(1)}, bf16[1,128,4,128]{1,0,3,2:T(2,128)(2,1)S(1)}, bf16[1,128,4,128]{1,0,3,2:T(2,128)(2,1)S(1)}) fusion(bf16[4,128,4,128]{1,0,3,2:T(4,128)(2,1)S(1)} %reshape.767, s32[]{:T(128)S(6)} %select_n.83, s32[]{:T(128)S(6)} %select_n.87, ...), kind=kLoop, calls=%fused_computation.181 | loop fusion | bytes 1048592 | tf_op jit(solution)/shard_map/jit(_take) | solution.py:39
  112.0 1.2 collective-permute-start.28
  113.4 2.3 %collective-permute-done.29 = bf16[128,4,128]{0,1,2:T(4,128)(2,1)S(1)} collective-permute-done((bf16[128,4,128]{0,1,2:T(4,128)(2,1)S(1)}, bf16[128,4,128]{0,1,2:T(4,128)(2,1)S(1)}, u32[]{:S(2)}, u32[]{:S(2)}) %collective-permute-start.29) | collective-permute-done | bytes 131104 | tf_op jit(solution)/shard_map/ppermute | solution.py:46
  115.7 4.2 %collective-permute-done.28 = bf16[128,4,128]{0,1,2:T(4,128)(2,1)S(1)} collective-permute-done((bf16[128,4,128]{0,1,2:T(4,128)(2,1)S(1)}, bf16[128,4,128]{0,1,2:T(4,128)(2,1)S(1)}, u32[]{:S(2)}, u32[]{:S(2)}) %collective-permute-start.28) | collective-permute-done | bytes 131104 | tf_op jit(solution)/shard_map/ppermute | solution.py:46
  (114 shorter events, 23.4 us)
Async XLA Ops:
  0.0 11.5 %copy-start = (bf16[3,128,512]{2,1,0:T(8,128)(2,1)S(1)}, bf16[3,128,512]{2,1,0:T(8,128)(2,1)}, u32[]{:S(2)}) copy-start(bf16[3,128,512]{2,1,0:T(8,128)(2,1)} %param.12) | copy-start | bytes 1179652
  12.1 10.4 %collective-permute-start.2 = (bf16[2,2,64,4,128]{4,2,3,1,0:T(8,128)(2,1)S(1)}, bf16[2,2,64,4,128]{4,2,3,1,0:T(8,128)(2,1)S(1)}, u32[]{:S(2)}, u32[]{:S(2)}) collective-permute-start(bf16[2,2,64,4,128]{4,2,3,1,0:T(8,128)(2,1)S(1)} %pad_maximum_fusion.1), channel_id=1, source_target_pairs={{0,12},{4,0},{8,4},{12,8},{1,13},{5,1},{9,5},{13,9},{2,14},{6,2},{... | collective-permute-start | bytes 786440 | tf_op jit(solution)/shard_map/ppermute | solution.py:78
  15.8 22.8 %collective-permute-start.1 = (bf16[2,2,64,4,128]{4,2,3,1,0:T(8,128)(2,1)S(1)}, bf16[2,2,64,4,128]{4,2,3,1,0:T(8,128)(2,1)S(1)}, u32[]{:S(2)}, u32[]{:S(2)}) collective-permute-start(bf16[2,2,64,4,128]{4,2,3,1,0:T(8,128)(2,1)S(1)} %pad_maximum_fusion.1), channel_id=1, source_target_pairs={{0,8},{4,12},{8,0},{12,4},{1,9},{5,13},{9,1},{13,5},{2,10},{6,14},... | collective-permute-start | bytes 786440 | tf_op jit(solution)/shard_map/ppermute | solution.py:78
  15.8 22.8 %collective-permute-start = (bf16[2,2,64,4,128]{4,2,3,1,0:T(8,128)(2,1)S(1)}, bf16[2,2,64,4,128]{4,2,3,1,0:T(8,128)(2,1)S(1)}, u32[]{:S(2)}, u32[]{:S(2)}) collective-permute-start(bf16[2,2,64,4,128]{4,2,3,1,0:T(8,128)(2,1)S(1)} %pad_maximum_fusion.1), channel_id=1, source_target_pairs={{0,4},{4,8},{8,12},{12,0},{1,5},{5,9},{9,13},{13,1},{2,6},{6,10},{... | collective-permute-start | bytes 786440 | tf_op jit(solution)/shard_map/ppermute | solution.py:78
  16.9 31.1 %collective-permute-start.11 = (bf16[128,4,1]{0,1,2:T(4,128)(2,1)S(1)}, bf16[128,4,1]{0,1,2:T(4,128)(2,1)S(1)}, u32[]{:S(2)}, u32[]{:S(2)}) collective-permute-start(bf16[128,4,1]{0,1,2:T(4,128)(2,1)S(1)} %get-tuple-element.43), channel_id=1, source_target_pairs={{0,12},{4,0},{8,4},{12,8},{1,13},{5,1},{9,5},{13,9},{2,14},{6,2},{... | collective-permute-start | bytes 3080 | tf_op jit(solution)/shard_map/ppermute | solution.py:149
  42.3 7.2 %collective-permute-start.15 = (bf16[128,4,1]{0,1,2:T(4,128)(2,1)S(1)}, bf16[128,4,1]{0,1,2:T(4,128)(2,1)S(1)}, u32[]{:S(2)}, u32[]{:S(2)}) collective-permute-start(bf16[128,4,1]{0,1,2:T(4,128)(2,1)S(1)} %get-tuple-element.51), channel_id=1, source_target_pairs={{0,15},{1,12},{2,13},{3,14},{4,3},{5,0},{6,1},{7,2},{8,7},{9,4},{1... | collective-permute-start | bytes 3080 | tf_op jit(solution)/shard_map/ppermute | solution.py:54
  42.6 8.8 %collective-permute-start.14 = (bf16[128,4,1]{0,1,2:T(4,128)(2,1)S(1)}, bf16[128,4,1]{0,1,2:T(4,128)(2,1)S(1)}, u32[]{:S(2)}, u32[]{:S(2)}) collective-permute-start(bf16[128,4,1]{0,1,2:T(4,128)(2,1)S(1)} %get-tuple-element.49), channel_id=1, source_target_pairs={{0,14},{1,15},{2,12},{3,13},{4,2},{5,3},{6,0},{7,1},{8,6},{9,7},{1... | collective-permute-start | bytes 3080 | tf_op jit(solution)/shard_map/ppermute | solution.py:54
  46.9 5.4 %collective-permute-start.13 = (bf16[128,4,1]{0,1,2:T(4,128)(2,1)S(1)}, bf16[128,4,1]{0,1,2:T(4,128)(2,1)S(1)}, u32[]{:S(2)}, u32[]{:S(2)}) collective-permute-start(bf16[128,4,1]{0,1,2:T(4,128)(2,1)S(1)} %get-tuple-element.47), channel_id=1, source_target_pairs={{0,13},{1,14},{2,15},{3,12},{4,1},{5,2},{6,3},{7,0},{8,5},{9,6},{1... | collective-permute-start | bytes 3080 | tf_op jit(solution)/shard_map/ppermute | solution.py:54
  47.2 5.7 %collective-permute-start.12 = (bf16[128,4,1]{0,1,2:T(4,128)(2,1)S(1)}, bf16[128,4,1]{0,1,2:T(4,128)(2,1)S(1)}, u32[]{:S(2)}, u32[]{:S(2)}) collective-permute-start(bf16[128,4,1]{0,1,2:T(4,128)(2,1)S(1)} %get-tuple-element.45), channel_id=1, source_target_pairs={{0,12},{1,13},{2,14},{3,15},{4,0},{5,1},{6,2},{7,3},{8,4},{9,5},{1... | collective-permute-start | bytes 3080 | tf_op jit(solution)/shard_map/ppermute | solution.py:54
  48.1 6.2 %collective-permute-start.6 = (bf16[128,4,1]{0,1,2:T(4,128)(2,1)S(1)}, bf16[128,4,1]{0,1,2:T(4,128)(2,1)S(1)}, u32[]{:S(2)}, u32[]{:S(2)}) collective-permute-start(bf16[128,4,1]{0,1,2:T(4,128)(2,1)S(1)} %get-tuple-element.42), channel_id=1, source_target_pairs={{0,4},{4,8},{8,12},{12,0},{1,5},{5,9},{9,13},{13,1},{2,6},{6,10},{... | collective-permute-start | bytes 3080 | tf_op jit(solution)/shard_map/ppermute | solution.py:146
  49.5 6.9 %collective-permute-start.10 = (bf16[128,4,1]{0,1,2:T(4,128)(2,1)S(1)}, bf16[128,4,1]{0,1,2:T(4,128)(2,1)S(1)}, u32[]{:S(2)}, u32[]{:S(2)}) collective-permute-start(bf16[128,4,1]{0,1,2:T(4,128)(2,1)S(1)} %get-tuple-element.50), channel_id=1, source_target_pairs={{0,7},{1,4},{2,5},{3,6},{4,11},{5,8},{6,9},{7,10},{8,15},{9,12},{1... | collective-permute-start | bytes 3080 | tf_op jit(solution)/shard_map/ppermute | solution.py:54
  51.4 6.3 %collective-permute-start.9 = (bf16[128,4,1]{0,1,2:T(4,128)(2,1)S(1)}, bf16[128,4,1]{0,1,2:T(4,128)(2,1)S(1)}, u32[]{:S(2)}, u32[]{:S(2)}) collective-permute-start(bf16[128,4,1]{0,1,2:T(4,128)(2,1)S(1)} %get-tuple-element.48), channel_id=1, source_target_pairs={{0,6},{1,7},{2,4},{3,5},{4,10},{5,11},{6,8},{7,9},{8,14},{9,15},{1... | collective-permute-start | bytes 3080 | tf_op jit(solution)/shard_map/ppermute | solution.py:54
  52.3 5.7 %collective-permute-start.8 = (bf16[128,4,1]{0,1,2:T(4,128)(2,1)S(1)}, bf16[128,4,1]{0,1,2:T(4,128)(2,1)S(1)}, u32[]{:S(2)}, u32[]{:S(2)}) collective-permute-start(bf16[128,4,1]{0,1,2:T(4,128)(2,1)S(1)} %get-tuple-element.46), channel_id=1, source_target_pairs={{0,5},{1,6},{2,7},{3,4},{4,9},{5,10},{6,11},{7,8},{8,13},{9,14},{1... | collective-permute-start | bytes 3080 | tf_op jit(solution)/shard_map/ppermute | solution.py:54
  52.9 5.4 %collective-permute-start.7 = (bf16[128,4,1]{0,1,2:T(4,128)(2,1)S(1)}, bf16[128,4,1]{0,1,2:T(4,128)(2,1)S(1)}, u32[]{:S(2)}, u32[]{:S(2)}) collective-permute-start(bf16[128,4,1]{0,1,2:T(4,128)(2,1)S(1)} %get-tuple-element.44), channel_id=1, source_target_pairs={{0,4},{1,5},{2,6},{3,7},{4,8},{5,9},{6,10},{7,11},{8,12},{9,13},{1... | collective-permute-start | bytes 3080 | tf_op jit(solution)/shard_map/ppermute | solution.py:54
  54.3 5.9 %collective-permute-start.5 = (bf16[128,4,128]{0,1,2:T(4,128)(2,1)S(1)}, bf16[128,4,128]{0,1,2:T(4,128)(2,1)S(1)}, u32[]{:S(2)}, u32[]{:S(2)}) collective-permute-start(bf16[128,4,128]{0,1,2:T(4,128)(2,1)S(1)} %fusion.109), channel_id=1, source_target_pairs={{0,3},{1,0},{2,1},{3,2},{4,7},{5,4},{6,5},{7,6},{8,11},{9,8},{10,9... | collective-permute-start | bytes 393224 | tf_op jit(solution)/shard_map/ppermute | solution.py:46
  56.4 7.8 %collective-permute-start.4 = (bf16[128,4,128]{0,1,2:T(4,128)(2,1)S(1)}, bf16[128,4,128]{0,1,2:T(4,128)(2,1)S(1)}, u32[]{:S(2)}, u32[]{:S(2)}) collective-permute-start(bf16[128,4,128]{0,1,2:T(4,128)(2,1)S(1)} %fusion.110), channel_id=1, source_target_pairs={{0,2},{1,3},{2,0},{3,1},{4,6},{5,7},{6,4},{7,5},{8,10},{9,11},{10,... | collective-permute-start | bytes 393224 | tf_op jit(solution)/shard_map/ppermute | solution.py:46
  57.7 6.5 %collective-permute-start.3 = (bf16[128,4,128]{0,1,2:T(4,128)(2,1)S(1)}, bf16[128,4,128]{0,1,2:T(4,128)(2,1)S(1)}, u32[]{:S(2)}, u32[]{:S(2)}) collective-permute-start(bf16[128,4,128]{0,1,2:T(4,128)(2,1)S(1)} %fusion.111), channel_id=1, source_target_pairs={{0,1},{1,2},{2,3},{3,0},{4,5},{5,6},{6,7},{7,4},{8,9},{9,10},{10,1... | collective-permute-start | bytes 393224 | tf_op jit(solution)/shard_map/ppermute | solution.py:46
  64.5 9.6 %copy-start.5 = (bf16[2,512,512]{2,1,0:T(8,128)(2,1)S(1)}, bf16[2,512,512]{2,1,0:T(8,128)(2,1)}, u32[]{:S(2)}) copy-start(bf16[2,512,512]{2,1,0:T(8,128)(2,1)} %param.17) | copy-start | bytes 3145732
  77.9 7.5 %collective-permute-start.26 = (bf16[128,4,1]{0,1,2:T(4,128)(2,1)S(1)}, bf16[128,4,1]{0,1,2:T(4,128)(2,1)S(1)}, u32[]{:S(2)}, u32[]{:S(2)}) collective-permute-start(bf16[128,4,1]{0,1,2:T(4,128)(2,1)S(1)} %get-tuple-element.41), channel_id=1, source_target_pairs={{0,15},{1,12},{2,13},{3,14},{4,3},{5,0},{6,1},{7,2},{8,7},{9,4},{1... | collective-permute-start | bytes 3080 | tf_op jit(solution)/shard_map/ppermute | solution.py:54
  80.8 5.5 %collective-permute-start.25 = (bf16[128,4,1]{0,1,2:T(4,128)(2,1)S(1)}, bf16[128,4,1]{0,1,2:T(4,128)(2,1)S(1)}, u32[]{:S(2)}, u32[]{:S(2)}) collective-permute-start(bf16[128,4,1]{0,1,2:T(4,128)(2,1)S(1)} %get-tuple-element.39), channel_id=1, source_target_pairs={{0,14},{1,15},{2,12},{3,13},{4,2},{5,3},{6,0},{7,1},{8,6},{9,7},{1... | collective-permute-start | bytes 3080 | tf_op jit(solution)/shard_map/ppermute | solution.py:54
  82.0 5.3 %collective-permute-start.24 = (bf16[128,4,1]{0,1,2:T(4,128)(2,1)S(1)}, bf16[128,4,1]{0,1,2:T(4,128)(2,1)S(1)}, u32[]{:S(2)}, u32[]{:S(2)}) collective-permute-start(bf16[128,4,1]{0,1,2:T(4,128)(2,1)S(1)} %get-tuple-element.37), channel_id=1, source_target_pairs={{0,13},{1,14},{2,15},{3,12},{4,1},{5,2},{6,3},{7,0},{8,5},{9,6},{1... | collective-permute-start | bytes 3080 | tf_op jit(solution)/shard_map/ppermute | solution.py:54
  82.9 5.8 %collective-permute-start.23 = (bf16[128,4,1]{0,1,2:T(4,128)(2,1)S(1)}, bf16[128,4,1]{0,1,2:T(4,128)(2,1)S(1)}, u32[]{:S(2)}, u32[]{:S(2)}) collective-permute-start(bf16[128,4,1]{0,1,2:T(4,128)(2,1)S(1)} %get-tuple-element.35), channel_id=1, source_target_pairs={{0,12},{1,13},{2,14},{3,15},{4,0},{5,1},{6,2},{7,3},{8,4},{9,5},{1... | collective-permute-start | bytes 3080 | tf_op jit(solution)/shard_map/ppermute | solution.py:54
  84.0 10.1 %collective-permute-start.18 = (bf16[128,4,128]{0,1,2:T(4,128)(2,1)S(1)}, bf16[128,4,128]{0,1,2:T(4,128)(2,1)S(1)}, u32[]{:S(2)}, u32[]{:S(2)}) collective-permute-start(bf16[128,4,128]{0,1,2:T(4,128)(2,1)S(1)} %fusion.104), channel_id=1, source_target_pairs={{0,3},{1,0},{2,1},{3,2},{4,7},{5,4},{6,5},{7,6},{8,11},{9,8},{10,9... | collective-permute-start | bytes 393224 | tf_op jit(solution)/shard_map/ppermute | solution.py:46
  85.4 4.9 %collective-permute-start.22 = (bf16[128,4,1]{0,1,2:T(4,128)(2,1)S(1)}, bf16[128,4,1]{0,1,2:T(4,128)(2,1)S(1)}, u32[]{:S(2)}, u32[]{:S(2)}) collective-permute-start(bf16[128,4,1]{0,1,2:T(4,128)(2,1)S(1)} %get-tuple-element.40), channel_id=1, source_target_pairs={{0,7},{1,4},{2,5},{3,6},{4,11},{5,8},{6,9},{7,10},{8,15},{9,12},{1... | collective-permute-start | bytes 3080 | tf_op jit(solution)/shard_map/ppermute | solution.py:54
  86.3 6.3 %collective-permute-start.21 = (bf16[128,4,1]{0,1,2:T(4,128)(2,1)S(1)}, bf16[128,4,1]{0,1,2:T(4,128)(2,1)S(1)}, u32[]{:S(2)}, u32[]{:S(2)}) collective-permute-start(bf16[128,4,1]{0,1,2:T(4,128)(2,1)S(1)} %get-tuple-element.38), channel_id=1, source_target_pairs={{0,6},{1,7},{2,4},{3,5},{4,10},{5,11},{6,8},{7,9},{8,14},{9,15},{1... | collective-permute-start | bytes 3080 | tf_op jit(solution)/shard_map/ppermute | solution.py:54
  87.3 5.7 %collective-permute-start.20 = (bf16[128,4,1]{0,1,2:T(4,128)(2,1)S(1)}, bf16[128,4,1]{0,1,2:T(4,128)(2,1)S(1)}, u32[]{:S(2)}, u32[]{:S(2)}) collective-permute-start(bf16[128,4,1]{0,1,2:T(4,128)(2,1)S(1)} %get-tuple-element.36), channel_id=1, source_target_pairs={{0,5},{1,6},{2,7},{3,4},{4,9},{5,10},{6,11},{7,8},{8,13},{9,14},{1... | collective-permute-start | bytes 3080 | tf_op jit(solution)/shard_map/ppermute | solution.py:54
  88.7 5.4 %collective-permute-start.19 = (bf16[128,4,1]{0,1,2:T(4,128)(2,1)S(1)}, bf16[128,4,1]{0,1,2:T(4,128)(2,1)S(1)}, u32[]{:S(2)}, u32[]{:S(2)}) collective-permute-start(bf16[128,4,1]{0,1,2:T(4,128)(2,1)S(1)} %get-tuple-element.34), channel_id=1, source_target_pairs={{0,4},{1,5},{2,6},{3,7},{4,8},{5,9},{6,10},{7,11},{8,12},{9,13},{1... | collective-permute-start | bytes 3080 | tf_op jit(solution)/shard_map/ppermute | solution.py:54
  90.4 6.1 %collective-permute-start.17 = (bf16[128,4,128]{0,1,2:T(4,128)(2,1)S(1)}, bf16[128,4,128]{0,1,2:T(4,128)(2,1)S(1)}, u32[]{:S(2)}, u32[]{:S(2)}) collective-permute-start(bf16[128,4,128]{0,1,2:T(4,128)(2,1)S(1)} %fusion.105), channel_id=1, source_target_pairs={{0,2},{1,3},{2,0},{3,1},{4,6},{5,7},{6,4},{7,5},{8,10},{9,11},{10,... | collective-permute-start | bytes 393224 | tf_op jit(solution)/shard_map/ppermute | solution.py:46
  92.6 4.9 %collective-permute-start.16 = (bf16[128,4,128]{0,1,2:T(4,128)(2,1)S(1)}, bf16[128,4,128]{0,1,2:T(4,128)(2,1)S(1)}, u32[]{:S(2)}, u32[]{:S(2)}) collective-permute-start(bf16[128,4,128]{0,1,2:T(4,128)(2,1)S(1)} %fusion.106), channel_id=1, source_target_pairs={{0,1},{1,2},{2,3},{3,0},{4,5},{5,6},{6,7},{7,4},{8,9},{9,10},{10,1... | collective-permute-start | bytes 393224 | tf_op jit(solution)/shard_map/ppermute | solution.py:46
  110.8 4.8 %collective-permute-start.29 = (bf16[128,4,128]{0,1,2:T(4,128)(2,1)S(1)}, bf16[128,4,128]{0,1,2:T(4,128)(2,1)S(1)}, u32[]{:S(2)}, u32[]{:S(2)}) collective-permute-start(bf16[128,4,128]{0,1,2:T(4,128)(2,1)S(1)} %fusion.99), channel_id=1, source_target_pairs={{0,3},{1,0},{2,1},{3,2},{4,7},{5,4},{6,5},{7,6},{8,11},{9,8},{10,9... | collective-permute-start | bytes 393224 | tf_op jit(solution)/shard_map/ppermute | solution.py:46
  112.0 7.9 %collective-permute-start.28 = (bf16[128,4,128]{0,1,2:T(4,128)(2,1)S(1)}, bf16[128,4,128]{0,1,2:T(4,128)(2,1)S(1)}, u32[]{:S(2)}, u32[]{:S(2)}) collective-permute-start(bf16[128,4,128]{0,1,2:T(4,128)(2,1)S(1)} %fusion.100), channel_id=1, source_target_pairs={{0,2},{1,3},{2,0},{3,1},{4,6},{5,7},{6,4},{7,5},{8,10},{9,11},{10,... | collective-permute-start | bytes 393224 | tf_op jit(solution)/shard_map/ppermute | solution.py:46
  113.3 6.6 %collective-permute-start.27 = (bf16[128,4,128]{0,1,2:T(4,128)(2,1)S(1)}, bf16[128,4,128]{0,1,2:T(4,128)(2,1)S(1)}, u32[]{:S(2)}, u32[]{:S(2)}) collective-permute-start(bf16[128,4,128]{0,1,2:T(4,128)(2,1)S(1)} %fusion.101), channel_id=1, source_target_pairs={{0,1},{1,2},{2,3},{3,0},{4,5},{5,6},{6,7},{7,4},{8,9},{9,10},{10,1... | collective-permute-start | bytes 393224 | tf_op jit(solution)/shard_map/ppermute | solution.py:46
  (4 other events, 21.9 us)
where the time goes:
time: 121 us
  waiting for transfers between devices  37.7 us (31%)
  starting transfers between devices  37.1 us (31%)
  blocking collectives  22.5 us (19%)
  other arithmetic  11.1 us (9%)
  local copies, waits for them, and re-layouts  6.3 us (5%)
  matrix products  5.77 us (5%)
    all_gather x3, blocking collectives, gather_channels(): return lax.all_gather(values, 'lev', axis=0, tiled=True)  22.5 us
    ppermute x16, starting transfers between devices, scatter_sum(): got = lax.ppermute(edge, ('lon', axis), pairs).astype(jnp.float32)  20.2 us
    ppermute x3, waiting for transfers between devices, gather_strips(): pieces.append(lax.ppermute(values, axis, pairs))  18.5 us
    ppermute x9, waiting for transfers between devices, scatter_sum(): total = total + lax.ppermute(chunk, axis, pairs).astype(jnp.float32)  15.8 us
    ppermute x9, starting transfers between devices, scatter_sum(): total = total + lax.ppermute(chunk, axis, pairs).astype(jnp.float32)  7.84 us
    ppermute x3, starting transfers between devices, gather_strips(): pieces.append(lax.ppermute(values, axis, pairs))  4.67 us
    dot_general x3, matrix products, spread_sum(): lax.dot_general(weight, activation, (((0,), (0,)), ((), ())), preferred_e...  4.29 us
    another operation x3, local copies, waits for them, and re-layouts, scatter_sum(): total = jnp.take(blocks, me, axis=0).astype(jnp.float32)  4.17 us
  transfers between devices with their start and end apart: 30, of which 14 were waited for; matrix products, arithmetic and copies ran while one was open for 4% of the time, Pallas kernels for 0%

commit v1 on v0

--- a/solution.py
+++ b/solution.py
@@ -28,7 +28,19 @@
 
 
 def gather_channels(values):
-    return lax.all_gather(values, "lev", axis=0, tiled=True)
+
+    def end_the_yards(content):
+        x_next = lax.axis_index("lev")
+        carry = lax.axis_size("lev")
+        prior, right_arr, o_now = (carry, x_next, content.shape[0])
+        r1, z1 = (content, 1)
+        while z1 < prior:
+            t_next = lax.ppermute(r1, "lev", [(it, (it - z1) % prior) for it in range(prior)])
+            r1 = jnp.concatenate([r1, t_next], axis=0)
+            z1 = 2 * z1
+        return jnp.roll(r1, right_arr * o_now, axis=0)
+
+    return end_the_yards(values)
 
 
 def scatter_sum(partial, axis, halo=False):

time: 121 us -> 145 us (1.20)
  blocking collectives: 22.5 us -> 0 us
  starting transfers between devices: 37.1 us -> 55.2 us
  waiting for transfers between devices: 37.7 us -> 55.4 us
  other arithmetic: 11.1 us -> 19.3 us
  local copies, waits for them, and re-layouts: 6.3 us -> 8.14 us
    ppermute x0 -> x6, waiting for transfers between devices: none -> 26.8 us  [end_the_yards(): lax.ppermute(r1, 'lev', [(it, (it - z1) % prior) for it in range(prior)])]
    all_gather x3 -> x0, blocking collectives: 22.5 us -> none  [gather_channels(): return lax.all_gather(values, 'lev', axis=0, tiled=True)]
    ppermute x0 -> x6, starting transfers between devices: none -> 9.21 us  [end_the_yards(): lax.ppermute(r1, 'lev', [(it, (it - z1) % prior) for it in range(prior)])]
    reduce_sum x3, other arithmetic: 1.65 us -> 10.8 us  [norm_channels(): jnp.mean(values * values, axis=0, keepdims=True) + epsilon]
    ppermute x16, starting transfers between devices: 20.2 us -> 26.7 us  [scatter_sum(): got = lax.ppermute(edge, ('lon', axis), pairs).astype(jnp.float32)]
    ppermute x16, waiting for transfers between devices: 3.41 us -> 0.04 us  [scatter_sum(): got = lax.ppermute(edge, ('lon', axis), pairs).astype(jnp.float32)]
    ppermute x9, waiting for transfers between devices: 15.8 us -> 12.8 us  [scatter_sum(): total = total + lax.ppermute(chunk, axis, pairs).astype(jnp.float32)]
    ppermute x3, waiting for transfers between devices: 18.5 us -> 15.7 us  [gather_strips(): pieces.append(lax.ppermute(values, axis, pairs))]
  transfers between devices with their start and end apart: 30 -> 36, of which waited for: 14 -> 15; matrix products, arithmetic and copies ran while one was open for 4% -> 13% of each run, Pallas kernels for 0% -> 0%
where the time goes in v1:
time: 145 us; the launch traced here: 144 us
  waiting for transfers between devices  55.4 us (38%)
  starting transfers between devices  55.2 us (38%)
  other arithmetic  19.3 us (13%)
  local copies, waits for them, and re-layouts  8.14 us (6%)
  matrix products  5.73 us (4%)
    ppermute x6, waiting for transfers between devices, end_the_yards(): lax.ppermute(r1, 'lev', [(it, (it - z1) % prior) for it in range(prior)])  26.8 us
    ppermute x16, starting transfers between devices, scatter_sum(): got = lax.ppermute(edge, ('lon', axis), pairs).astype(jnp.float32)  26.7 us
    ppermute x3, waiting for transfers between devices, gather_strips(): pieces.append(lax.ppermute(values, axis, pairs))  15.7 us
    ppermute x9, waiting for transfers between devices, scatter_sum(): total = total + lax.ppermute(chunk, axis, pairs).astype(jnp.float32)  12.8 us
    reduce_sum x3, other arithmetic, norm_channels(): jnp.mean(values * values, axis=0, keepdims=True) + epsilon  10.8 us
    ppermute x6, starting transfers between devices, end_the_yards(): lax.ppermute(r1, 'lev', [(it, (it - z1) % prior) for it in range(prior)])  9.21 us
    ppermute x9, starting transfers between devices, scatter_sum(): total = total + lax.ppermute(chunk, axis, pairs).astype(jnp.float32)  8.29 us
    ppermute x3, starting transfers between devices, gather_strips(): pieces.append(lax.ppermute(values, axis, pairs))  5.57 us
  transfers between devices with their start and end apart: 36, of which 15 were waited for; matrix products, arithmetic and copies ran while one was open for 13% of the time, Pallas kernels for 0%

profile of v1, /device:TPU:0, one launch (start us, length us, event | category | flops | bytes accessed | tf_op | source)
XLA Modules:
  0.0 144.3 jit_solution(10045885630686537973)
XLA Ops:
  0.0 2.4 %collective-permute-start = (bf16[128,4,128]{2,1,0:T(4,128)(2,1)}, bf16[128,4,128]{2,1,0:T(4,128)(2,1)S(1)}, u32[]{:S(2)}, u32[]{:S(2)}) collective-permute-start(bf16[128,4,128]{2,1,0:T(4,128)(2,1)} %param.12), channel_id=1, source_target_pairs={{0,3},{1,0},{2,1},{3,2},{4,7},{5,4},{6,5},{7,6},{8,11},{9,8},{10,9... | collective-permute-start | bytes 393224 | tf_op jit(solution)/shard_map/ppermute | solution.py:38
  3.5 1.6 %collective-permute-start.8 = (bf16[128,4,1]{0,1,2:T(4,128)(2,1)S(1)}, bf16[128,4,1]{0,1,2:T(4,128)(2,1)S(1)}, u32[]{:S(2)}, u32[]{:S(2)}) collective-permute-start(bf16[128,4,1]{0,1,2:T(4,128)(2,1)S(1)} %get-tuple-element.49), channel_id=1, source_target_pairs={{0,4},{4,8},{8,12},{12,0},{1,5},{5,9},{9,13},{13,1},{2,6},{6,10},{... | collective-permute-start | bytes 3080 | tf_op jit(solution)/shard_map/ppermute | solution.py:158
  7.9 7.3 %collective-permute-done.1 = bf16[256,4,128]{2,1,0:T(4,128)(2,1)S(1)} collective-permute-done((bf16[256,4,128]{2,1,0:T(4,128)(2,1)S(1)}, bf16[256,4,128]{2,1,0:T(4,128)(2,1)S(1)}, u32[]{:S(2)}, u32[]{:S(2)}) %collective-permute-start.1) | collective-permute-done | bytes 262176 | tf_op jit(solution)/shard_map/ppermute | solution.py:38
  15.3 7.3 %fusion.7 = (f32[4,128]{1,0:T(4,128)S(1)}, bf16[512,4,128]{2,1,0:T(4,128)(2,1)S(1)}) fusion(s32[]{:T(128)S(6)} %select_n.97, bf16[256,4,128]{2,1,0:T(4,128)(2,1)S(1)} %collective-permute-done.1, bf16[128,4,128]{2,1,0:T(4,128)(2,1)S(1)} %collective-permute-done, bf16[128,4,128]{2,1,0:T(4,128)(2,1)} %param.12), kind=kLoop, calls=%fused_computation.23 | loop fusion | flops 2096640 | bytes 1050628 | tf_op jit(solution)/shard_map/reduce_sum | solution.py:22
  22.6 1.9 %fusion.49 = bf16[512,4,128,1]{2,1,0,3:T(4,128)(2,1)S(1)} fusion(bf16[512,4,128]{2,1,0:T(4,128)(2,1)S(1)} %get-tuple-element.23, f32[512]{0:T(512)} %param.13, f32[4,128]{1,0:T(4,128)S(1)} %add_rsqrt_fusion.4), kind=kLoop, calls=%fused_computation.95 | loop fusion | flops 1048576 | bytes 1052672 | tf_op jit(solution)/shard_map/convert_element_type | solution.py:148
  25.2 1.6 %collective-permute-start.2 = (bf16[2,2,64,4,128]{4,2,3,1,0:T(8,128)(2,1)S(1)}, bf16[2,2,64,4,128]{4,2,3,1,0:T(8,128)(2,1)S(1)}, u32[]{:S(2)}, u32[]{:S(2)}) collective-permute-start(bf16[2,2,64,4,128]{4,2,3,1,0:T(8,128)(2,1)S(1)} %pad_maximum_fusion.2), channel_id=1, source_target_pairs={{0,4},{4,8},{8,12},{12,0},{1,5},{5,9},{9,13},{13,1},{2,6},{6,10},{... | collective-permute-start | bytes 786440 | tf_op jit(solution)/shard_map/ppermute | solution.py:90
  26.8 2.6 %collective-permute-start.3 = (bf16[2,2,64,4,128]{4,2,3,1,0:T(8,128)(2,1)S(1)}, bf16[2,2,64,4,128]{4,2,3,1,0:T(8,128)(2,1)S(1)}, u32[]{:S(2)}, u32[]{:S(2)}) collective-permute-start(bf16[2,2,64,4,128]{4,2,3,1,0:T(8,128)(2,1)S(1)} %pad_maximum_fusion.2), channel_id=1, source_target_pairs={{0,8},{4,12},{8,0},{12,4},{1,9},{5,13},{9,1},{13,5},{2,10},{6,14},... | collective-permute-start | bytes 786440 | tf_op jit(solution)/shard_map/ppermute | solution.py:90
  30.8 5.6 %collective-permute-done.2 = bf16[2,2,64,4,128]{4,2,3,1,0:T(8,128)(2,1)S(1)} collective-permute-done((bf16[2,2,64,4,128]{4,2,3,1,0:T(8,128)(2,1)S(1)}, bf16[2,2,64,4,128]{4,2,3,1,0:T(8,128)(2,1)S(1)}, u32[]{:S(2)}, u32[]{:S(2)}) %collective-permute-start.2) | collective-permute-done | bytes 262176 | tf_op jit(solution)/shard_map/ppermute | solution.py:90
  36.4 10.2 %collective-permute-done.3 = bf16[2,2,64,4,128]{4,2,3,1,0:T(8,128)(2,1)S(1)} collective-permute-done((bf16[2,2,64,4,128]{4,2,3,1,0:T(8,128)(2,1)S(1)}, bf16[2,2,64,4,128]{4,2,3,1,0:T(8,128)(2,1)S(1)}, u32[]{:S(2)}, u32[]{:S(2)}) %collective-permute-start.3) | collective-permute-done | bytes 262176 | tf_op jit(solution)/shard_map/ppermute | solution.py:90
  50.4 6.1 %collective-permute-start.9 = (bf16[128,4,1]{0,1,2:T(4,128)(2,1)S(1)}, bf16[128,4,1]{0,1,2:T(4,128)(2,1)S(1)}, u32[]{:S(2)}, u32[]{:S(2)}) collective-permute-start(bf16[128,4,1]{0,1,2:T(4,128)(2,1)S(1)} %get-tuple-element.51), channel_id=1, source_target_pairs={{0,4},{1,5},{2,6},{3,7},{4,8},{5,9},{6,10},{7,11},{8,12},{9,13},{1... | collective-permute-start | bytes 3080 | tf_op jit(solution)/shard_map/ppermute | solution.py:66
  58.6 1.6 %collective-permute-start.12 = (bf16[128,4,1]{0,1,2:T(4,128)(2,1)S(1)}, bf16[128,4,1]{0,1,2:T(4,128)(2,1)S(1)}, u32[]{:S(2)}, u32[]{:S(2)}) collective-permute-start(bf16[128,4,1]{0,1,2:T(4,128)(2,1)S(1)} %get-tuple-element.57), channel_id=1, source_target_pairs={{0,7},{1,4},{2,5},{3,6},{4,11},{5,8},{6,9},{7,10},{8,15},{9,12},{1... | collective-permute-start | bytes 3080 | tf_op jit(solution)/shard_map/ppermute | solution.py:66
  60.2 3.8 %collective-permute-start.13 = (bf16[128,4,1]{0,1,2:T(4,128)(2,1)S(1)}, bf16[128,4,1]{0,1,2:T(4,128)(2,1)S(1)}, u32[]{:S(2)}, u32[]{:S(2)}) collective-permute-start(bf16[128,4,1]{0,1,2:T(4,128)(2,1)S(1)} %get-tuple-element.50), channel_id=1, source_target_pairs={{0,12},{4,0},{8,4},{12,8},{1,13},{5,1},{9,5},{13,9},{2,14},{6,2},{... | collective-permute-start | bytes 3080 | tf_op jit(solution)/shard_map/ppermute | solution.py:161
  64.1 2.5 %collective-permute-start.16 = (bf16[128,4,1]{0,1,2:T(4,128)(2,1)S(1)}, bf16[128,4,1]{0,1,2:T(4,128)(2,1)S(1)}, u32[]{:S(2)}, u32[]{:S(2)}) collective-permute-start(bf16[128,4,1]{0,1,2:T(4,128)(2,1)S(1)} %get-tuple-element.56), channel_id=1, source_target_pairs={{0,14},{1,15},{2,12},{3,13},{4,2},{5,3},{6,0},{7,1},{8,6},{9,7},{1... | collective-permute-start | bytes 3080 | tf_op jit(solution)/shard_map/ppermute | solution.py:66
  66.6 3.3 %collective-permute-start.17 = (bf16[128,4,1]{0,1,2:T(4,128)(2,1)S(1)}, bf16[128,4,1]{0,1,2:T(4,128)(2,1)S(1)}, u32[]{:S(2)}, u32[]{:S(2)}) collective-permute-start(bf16[128,4,1]{0,1,2:T(4,128)(2,1)S(1)} %get-tuple-element.58), channel_id=1, source_target_pairs={{0,15},{1,12},{2,13},{3,14},{4,3},{5,0},{6,1},{7,2},{8,7},{9,4},{1... | collective-permute-start | bytes 3080 | tf_op jit(solution)/shard_map/ppermute | solution.py:66
  72.3 2.9 %collective-permute-done.5 = bf16[128,4,128]{0,1,2:T(4,128)(2,1)S(1)} collective-permute-done((bf16[128,4,128]{0,1,2:T(4,128)(2,1)S(1)}, bf16[128,4,128]{0,1,2:T(4,128)(2,1)S(1)}, u32[]{:S(2)}, u32[]{:S(2)}) %collective-permute-start.5) | collective-permute-done | bytes 131104 | tf_op jit(solution)/shard_map/ppermute | solution.py:58
  77.8 2.0 %collective-permute-start.18 = (bf16[128,4,128]{0,1,2:T(4,128)(2,1)S(1)}, bf16[128,4,128]{0,1,2:T(4,128)(2,1)S(1)}, u32[]{:S(2)}, u32[]{:S(2)}) collective-permute-start(bf16[128,4,128]{0,1,2:T(4,128)(2,1)S(1)} %fusion.103), channel_id=1, source_target_pairs={{0,3},{1,0},{2,1},{3,2},{4,7},{5,4},{6,5},{7,6},{8,11},{9,8},{10,9... | collective-permute-start | bytes 393224 | tf_op jit(solution)/shard_map/ppermute | solution.py:38
  79.7 2.5 %collective-permute-done.18 = bf16[128,4,128]{0,1,2:T(4,128)(2,1)S(1)} collective-permute-done((bf16[128,4,128]{0,1,2:T(4,128)(2,1)S(1)}, bf16[128,4,128]{0,1,2:T(4,128)(2,1)S(1)}, u32[]{:S(2)}, u32[]{:S(2)}) %collective-permute-start.18) | collective-permute-done | bytes 131104 | tf_op jit(solution)/shard_map/ppermute | solution.py:38
  83.7 7.5 %collective-permute-done.19 = bf16[256,4,128]{0,1,2:T(4,128)(2,1)S(1)} collective-permute-done((bf16[256,4,128]{0,1,2:T(4,128)(2,1)S(1)}, bf16[256,4,128]{0,1,2:T(4,128)(2,1)S(1)}, u32[]{:S(2)}, u32[]{:S(2)}) %collective-permute-start.19) | collective-permute-done | bytes 262176 | tf_op jit(solution)/shard_map/ppermute | solution.py:38
  91.2 1.7 %fusion.10 = (f32[4,128]{0,1:T(8,128)S(1)}, bf16[512,4,128]{0,1,2:T(4,128)(2,1)S(1)}) fusion(s32[]{:T(128)S(6)} %select_n.97, bf16[256,4,128]{0,1,2:T(4,128)(2,1)S(1)} %collective-permute-done.19, bf16[128,4,128]{0,1,2:T(4,128)(2,1)S(1)} %collective-permute-done.18, bf16[128,4,128]{0,1,2:T(4,128)(2,1)S(1)} %fusion.103), kind=kLoop, calls=%fused_computation.26 | loop fusion | flops 3931648 | bytes 1050628 | tf_op jit(solution)/shard_map/reduce_sum | solution.py:22
  93.4 2.0 %fusion.3 = bf16[512,512]{0,1:T(8,128)(2,1)S(1)} fusion(bf16[512,512]{0,1:T(8,128)(2,1)S(1)} %bitcast.151, bf16[2,512,512]{2,1,0:T(8,128)(2,1)S(1)} %copy-done.3, bf16[2,512,512]{2,1,0:T(8,128)(2,1)} %param.18), kind=kOutput, calls=%fused_computation.18 | convolution fusion | flops 539492352 | bytes 2097152 | tf_op jit(solution)/shard_map/dot_general | solution.py:75
  100.1 4.3 %collective-permute-start.26 = (bf16[128,4,1]{0,1,2:T(4,128)(2,1)S(1)}, bf16[128,4,1]{0,1,2:T(4,128)(2,1)S(1)}, u32[]{:S(2)}, u32[]{:S(2)}) collective-permute-start(bf16[128,4,1]{0,1,2:T(4,128)(2,1)S(1)} %get-tuple-element.47), channel_id=1, source_target_pairs={{0,7},{1,4},{2,5},{3,6},{4,11},{5,8},{6,9},{7,10},{8,15},{9,12},{1... | collective-permute-start | bytes 3080 | tf_op jit(solution)/shard_map/ppermute | solution.py:66
  104.5 1.7 %collective-permute-start.28 = (bf16[128,4,1]{0,1,2:T(4,128)(2,1)S(1)}, bf16[128,4,1]{0,1,2:T(4,128)(2,1)S(1)}, u32[]{:S(2)}, u32[]{:S(2)}) collective-permute-start(bf16[128,4,1]{0,1,2:T(4,128)(2,1)S(1)} %get-tuple-element.44), channel_id=1, source_target_pairs={{0,13},{1,14},{2,15},{3,12},{4,1},{5,2},{6,3},{7,0},{8,5},{9,6},{1... | collective-permute-start | bytes 3080 | tf_op jit(solution)/shard_map/ppermute | solution.py:66
  106.2 2.0 %collective-permute-start.29 = (bf16[128,4,1]{0,1,2:T(4,128)(2,1)S(1)}, bf16[128,4,1]{0,1,2:T(4,128)(2,1)S(1)}, u32[]{:S(2)}, u32[]{:S(2)}) collective-permute-start(bf16[128,4,1]{0,1,2:T(4,128)(2,1)S(1)} %get-tuple-element.46), channel_id=1, source_target_pairs={{0,14},{1,15},{2,12},{3,13},{4,2},{5,3},{6,0},{7,1},{8,6},{9,7},{1... | collective-permute-start | bytes 3080 | tf_op jit(solution)/shard_map/ppermute | solution.py:66
  109.6 1.6 %collective-permute-start.21 = (bf16[128,4,128]{0,1,2:T(4,128)(2,1)S(1)}, bf16[128,4,128]{0,1,2:T(4,128)(2,1)S(1)}, u32[]{:S(2)}, u32[]{:S(2)}) collective-permute-start(bf16[128,4,128]{0,1,2:T(4,128)(2,1)S(1)} %fusion.112), channel_id=1, source_target_pairs={{0,2},{1,3},{2,0},{3,1},{4,6},{5,7},{6,4},{7,5},{8,10},{9,11},{10,... | collective-permute-start | bytes 393224 | tf_op jit(solution)/shard_map/ppermute | solution.py:58
  111.9 4.0 %collective-permute-done.21 = bf16[128,4,128]{0,1,2:T(4,128)(2,1)S(1)} collective-permute-done((bf16[128,4,128]{0,1,2:T(4,128)(2,1)S(1)}, bf16[128,4,128]{0,1,2:T(4,128)(2,1)S(1)}, u32[]{:S(2)}, u32[]{:S(2)}) %collective-permute-start.21) | collective-permute-done | bytes 131104 | tf_op jit(solution)/shard_map/ppermute | solution.py:58
  118.0 2.5 %collective-permute-done.31 = bf16[128,4,128]{0,1,2:T(4,128)(2,1)S(1)} collective-permute-done((bf16[128,4,128]{0,1,2:T(4,128)(2,1)S(1)}, bf16[128,4,128]{0,1,2:T(4,128)(2,1)S(1)}, u32[]{:S(2)}, u32[]{:S(2)}) %collective-permute-start.31) | collective-permute-done | bytes 131104 | tf_op jit(solution)/shard_map/ppermute | solution.py:38
  120.7 1.6 %collective-permute-start.32 = (bf16[256,4,128]{0,1,2:T(4,128)(2,1)S(1)}, bf16[256,4,128]{0,1,2:T(4,128)(2,1)S(1)}, u32[]{:S(2)}, u32[]{:S(2)}) collective-permute-start(bf16[256,4,128]{0,1,2:T(4,128)(2,1)S(1)} %pad_maximum_fusion.4), channel_id=1, source_target_pairs={{0,2},{1,3},{2,0},{3,1},{4,6},{5,7},{6,4},{7,5},{8,10},{9,11},{10,... | collective-permute-start | bytes 786440 | tf_op jit(solution)/shard_map/ppermute | solution.py:38
  122.3 6.8 %collective-permute-done.32 = bf16[256,4,128]{0,1,2:T(4,128)(2,1)S(1)} collective-permute-done((bf16[256,4,128]{0,1,2:T(4,128)(2,1)S(1)}, bf16[256,4,128]{0,1,2:T(4,128)(2,1)S(1)}, u32[]{:S(2)}, u32[]{:S(2)}) %collective-permute-start.32) | collective-permute-done | bytes 262176 | tf_op jit(solution)/shard_map/ppermute | solution.py:38
  129.1 1.7 %fusion.13 = (f32[4,128]{0,1:T(8,128)S(1)}, bf16[512,4,128]{0,1,2:T(4,128)(2,1)S(1)}) fusion(s32[]{:T(128)S(6)} %select_n.97, bf16[256,4,128]{0,1,2:T(4,128)(2,1)S(1)} %collective-permute-done.32, bf16[128,4,128]{0,1,2:T(4,128)(2,1)S(1)} %collective-permute-done.31, bf16[128,4,128]{0,1,2:T(4,128)(2,1)S(1)} %fusion.102), kind=kLoop, calls=%fused_computation.29 | loop fusion | flops 3931648 | bytes 1050628 | tf_op jit(solution)/shard_map/reduce_sum | solution.py:22
  131.3 2.0 %fusion.4 = bf16[512,512]{0,1:T(8,128)(2,1)S(1)} fusion(bf16[512,512]{0,1:T(8,128)(2,1)S(1)} %bitcast.152, bf16[2,512,512]{2,1,0:T(8,128)(2,1)S(1)} %copy-done.3, bf16[2,512,512]{2,1,0:T(8,128)(2,1)} %param.18), kind=kOutput, calls=%fused_computation.19 | convolution fusion | flops 539492352 | bytes 2097152 | tf_op jit(solution)/shard_map/dot_general | solution.py:75
  135.8 1.6 %collective-permute-start.34 = (bf16[128,4,128]{0,1,2:T(4,128)(2,1)S(1)}, bf16[128,4,128]{0,1,2:T(4,128)(2,1)S(1)}, u32[]{:S(2)}, u32[]{:S(2)}) collective-permute-start(bf16[128,4,128]{0,1,2:T(4,128)(2,1)S(1)} %fusion.107), channel_id=1, source_target_pairs={{0,2},{1,3},{2,0},{3,1},{4,6},{5,7},{6,4},{7,5},{8,10},{9,11},{10,... | collective-permute-start | bytes 393224 | tf_op jit(solution)/shard_map/ppermute | solution.py:58
  139.3 2.3 %collective-permute-done.34 = bf16[128,4,128]{0,1,2:T(4,128)(2,1)S(1)} collective-permute-done((bf16[128,4,128]{0,1,2:T(4,128)(2,1)S(1)}, bf16[128,4,128]{0,1,2:T(4,128)(2,1)S(1)}, u32[]{:S(2)}, u32[]{:S(2)}) %collective-permute-start.34) | collective-permute-done | bytes 131104 | tf_op jit(solution)/shard_map/ppermute | solution.py:58
  (122 shorter events, 34.9 us)
Async XLA Ops:
  0.0 5.2 %collective-permute-start = (bf16[128,4,128]{2,1,0:T(4,128)(2,1)}, bf16[128,4,128]{2,1,0:T(4,128)(2,1)S(1)}, u32[]{:S(2)}, u32[]{:S(2)}) collective-permute-start(bf16[128,4,128]{2,1,0:T(4,128)(2,1)} %param.12), channel_id=1, source_target_pairs={{0,3},{1,0},{2,1},{3,2},{4,7},{5,4},{6,5},{7,6},{8,11},{9,8},{10,9... | collective-permute-start | bytes 393224 | tf_op jit(solution)/shard_map/ppermute | solution.py:38
  3.5 56.7 %collective-permute-start.8 = (bf16[128,4,1]{0,1,2:T(4,128)(2,1)S(1)}, bf16[128,4,1]{0,1,2:T(4,128)(2,1)S(1)}, u32[]{:S(2)}, u32[]{:S(2)}) collective-permute-start(bf16[128,4,1]{0,1,2:T(4,128)(2,1)S(1)} %get-tuple-element.49), channel_id=1, source_target_pairs={{0,4},{4,8},{8,12},{12,0},{1,5},{5,9},{9,13},{13,1},{2,6},{6,10},{... | collective-permute-start | bytes 3080 | tf_op jit(solution)/shard_map/ppermute | solution.py:158
  6.3 9.0 %collective-permute-start.1 = (bf16[256,4,128]{2,1,0:T(4,128)(2,1)S(1)}, bf16[256,4,128]{2,1,0:T(4,128)(2,1)S(1)}, u32[]{:S(2)}, u32[]{:S(2)}) collective-permute-start(bf16[256,4,128]{2,1,0:T(4,128)(2,1)S(1)} %pad_maximum_fusion.1), channel_id=1, source_target_pairs={{0,2},{1,3},{2,0},{3,1},{4,6},{5,7},{6,4},{7,5},{8,10},{9,11},{10,... | collective-permute-start | bytes 786440 | tf_op jit(solution)/shard_map/ppermute | solution.py:38
  25.2 11.2 %collective-permute-start.2 = (bf16[2,2,64,4,128]{4,2,3,1,0:T(8,128)(2,1)S(1)}, bf16[2,2,64,4,128]{4,2,3,1,0:T(8,128)(2,1)S(1)}, u32[]{:S(2)}, u32[]{:S(2)}) collective-permute-start(bf16[2,2,64,4,128]{4,2,3,1,0:T(8,128)(2,1)S(1)} %pad_maximum_fusion.2), channel_id=1, source_target_pairs={{0,4},{4,8},{8,12},{12,0},{1,5},{5,9},{9,13},{13,1},{2,6},{6,10},{... | collective-permute-start | bytes 786440 | tf_op jit(solution)/shard_map/ppermute | solution.py:90
  26.8 19.7 %collective-permute-start.3 = (bf16[2,2,64,4,128]{4,2,3,1,0:T(8,128)(2,1)S(1)}, bf16[2,2,64,4,128]{4,2,3,1,0:T(8,128)(2,1)S(1)}, u32[]{:S(2)}, u32[]{:S(2)}) collective-permute-start(bf16[2,2,64,4,128]{4,2,3,1,0:T(8,128)(2,1)S(1)} %pad_maximum_fusion.2), channel_id=1, source_target_pairs={{0,8},{4,12},{8,0},{12,4},{1,9},{5,13},{9,1},{13,5},{2,10},{6,14},... | collective-permute-start | bytes 786440 | tf_op jit(solution)/shard_map/ppermute | solution.py:90
  29.4 17.1 %collective-permute-start.4 = (bf16[2,2,64,4,128]{4,2,3,1,0:T(8,128)(2,1)S(1)}, bf16[2,2,64,4,128]{4,2,3,1,0:T(8,128)(2,1)S(1)}, u32[]{:S(2)}, u32[]{:S(2)}) collective-permute-start(bf16[2,2,64,4,128]{4,2,3,1,0:T(8,128)(2,1)S(1)} %pad_maximum_fusion.2), channel_id=1, source_target_pairs={{0,12},{4,0},{8,4},{12,8},{1,13},{5,1},{9,5},{13,9},{2,14},{6,2},{... | collective-permute-start | bytes 786440 | tf_op jit(solution)/shard_map/ppermute | solution.py:90
  50.4 13.6 %collective-permute-start.9 = (bf16[128,4,1]{0,1,2:T(4,128)(2,1)S(1)}, bf16[128,4,1]{0,1,2:T(4,128)(2,1)S(1)}, u32[]{:S(2)}, u32[]{:S(2)}) collective-permute-start(bf16[128,4,1]{0,1,2:T(4,128)(2,1)S(1)} %get-tuple-element.51), channel_id=1, source_target_pairs={{0,4},{1,5},{2,6},{3,7},{4,8},{5,9},{6,10},{7,11},{8,12},{9,13},{1... | collective-permute-start | bytes 3080 | tf_op jit(solution)/shard_map/ppermute | solution.py:66
  56.8 7.3 %collective-permute-start.10 = (bf16[128,4,1]{0,1,2:T(4,128)(2,1)S(1)}, bf16[128,4,1]{0,1,2:T(4,128)(2,1)S(1)}, u32[]{:S(2)}, u32[]{:S(2)}) collective-permute-start(bf16[128,4,1]{0,1,2:T(4,128)(2,1)S(1)} %get-tuple-element.53), channel_id=1, source_target_pairs={{0,5},{1,6},{2,7},{3,4},{4,9},{5,10},{6,11},{7,8},{8,13},{9,14},{1... | collective-permute-start | bytes 3080 | tf_op jit(solution)/shard_map/ppermute | solution.py:66
  57.1 7.1 %collective-permute-start.11 = (bf16[128,4,1]{0,1,2:T(4,128)(2,1)S(1)}, bf16[128,4,1]{0,1,2:T(4,128)(2,1)S(1)}, u32[]{:S(2)}, u32[]{:S(2)}) collective-permute-start(bf16[128,4,1]{0,1,2:T(4,128)(2,1)S(1)} %get-tuple-element.55), channel_id=1, source_target_pairs={{0,6},{1,7},{2,4},{3,5},{4,10},{5,11},{6,8},{7,9},{8,14},{9,15},{1... | collective-permute-start | bytes 3080 | tf_op jit(solution)/shard_map/ppermute | solution.py:66
  58.6 8.1 %collective-permute-start.12 = (bf16[128,4,1]{0,1,2:T(4,128)(2,1)S(1)}, bf16[128,4,1]{0,1,2:T(4,128)(2,1)S(1)}, u32[]{:S(2)}, u32[]{:S(2)}) collective-permute-start(bf16[128,4,1]{0,1,2:T(4,128)(2,1)S(1)} %get-tuple-element.57), channel_id=1, source_target_pairs={{0,7},{1,4},{2,5},{3,6},{4,11},{5,8},{6,9},{7,10},{8,15},{9,12},{1... | collective-permute-start | bytes 3080 | tf_op jit(solution)/shard_map/ppermute | solution.py:66
  60.2 9.8 %collective-permute-start.13 = (bf16[128,4,1]{0,1,2:T(4,128)(2,1)S(1)}, bf16[128,4,1]{0,1,2:T(4,128)(2,1)S(1)}, u32[]{:S(2)}, u32[]{:S(2)}) collective-permute-start(bf16[128,4,1]{0,1,2:T(4,128)(2,1)S(1)} %get-tuple-element.50), channel_id=1, source_target_pairs={{0,12},{4,0},{8,4},{12,8},{1,13},{5,1},{9,5},{13,9},{2,14},{6,2},{... | collective-permute-start | bytes 3080 | tf_op jit(solution)/shard_map/ppermute | solution.py:161
  64.0 6.0 %collective-permute-start.14 = (bf16[128,4,1]{0,1,2:T(4,128)(2,1)S(1)}, bf16[128,4,1]{0,1,2:T(4,128)(2,1)S(1)}, u32[]{:S(2)}, u32[]{:S(2)}) collective-permute-start(bf16[128,4,1]{0,1,2:T(4,128)(2,1)S(1)} %get-tuple-element.52), channel_id=1, source_target_pairs={{0,12},{1,13},{2,14},{3,15},{4,0},{5,1},{6,2},{7,3},{8,4},{9,5},{1... | collective-permute-start | bytes 3080 | tf_op jit(solution)/shard_map/ppermute | solution.py:66
  64.1 6.8 %collective-permute-start.15 = (bf16[128,4,1]{0,1,2:T(4,128)(2,1)S(1)}, bf16[128,4,1]{0,1,2:T(4,128)(2,1)S(1)}, u32[]{:S(2)}, u32[]{:S(2)}) collective-permute-start(bf16[128,4,1]{0,1,2:T(4,128)(2,1)S(1)} %get-tuple-element.54), channel_id=1, source_target_pairs={{0,13},{1,14},{2,15},{3,12},{4,1},{5,2},{6,3},{7,0},{8,5},{9,6},{1... | collective-permute-start | bytes 3080 | tf_op jit(solution)/shard_map/ppermute | solution.py:66
  64.1 8.2 %collective-permute-start.16 = (bf16[128,4,1]{0,1,2:T(4,128)(2,1)S(1)}, bf16[128,4,1]{0,1,2:T(4,128)(2,1)S(1)}, u32[]{:S(2)}, u32[]{:S(2)}) collective-permute-start(bf16[128,4,1]{0,1,2:T(4,128)(2,1)S(1)} %get-tuple-element.56), channel_id=1, source_target_pairs={{0,14},{1,15},{2,12},{3,13},{4,2},{5,3},{6,0},{7,1},{8,6},{9,7},{1... | collective-permute-start | bytes 3080 | tf_op jit(solution)/shard_map/ppermute | solution.py:66
  66.6 5.7 %collective-permute-start.17 = (bf16[128,4,1]{0,1,2:T(4,128)(2,1)S(1)}, bf16[128,4,1]{0,1,2:T(4,128)(2,1)S(1)}, u32[]{:S(2)}, u32[]{:S(2)}) collective-permute-start(bf16[128,4,1]{0,1,2:T(4,128)(2,1)S(1)} %get-tuple-element.58), channel_id=1, source_target_pairs={{0,15},{1,12},{2,13},{3,14},{4,3},{5,0},{6,1},{7,2},{8,7},{9,4},{1... | collective-permute-start | bytes 3080 | tf_op jit(solution)/shard_map/ppermute | solution.py:66
  70.0 5.2 %collective-permute-start.5 = (bf16[128,4,128]{0,1,2:T(4,128)(2,1)S(1)}, bf16[128,4,128]{0,1,2:T(4,128)(2,1)S(1)}, u32[]{:S(2)}, u32[]{:S(2)}) collective-permute-start(bf16[128,4,128]{0,1,2:T(4,128)(2,1)S(1)} %fusion.118), channel_id=1, source_target_pairs={{0,1},{1,2},{2,3},{3,0},{4,5},{5,6},{6,7},{7,4},{8,9},{9,10},{10,1... | collective-permute-start | bytes 393224 | tf_op jit(solution)/shard_map/ppermute | solution.py:58
  70.0 6.4 %collective-permute-start.6 = (bf16[128,4,128]{0,1,2:T(4,128)(2,1)S(1)}, bf16[128,4,128]{0,1,2:T(4,128)(2,1)S(1)}, u32[]{:S(2)}, u32[]{:S(2)}) collective-permute-start(bf16[128,4,128]{0,1,2:T(4,128)(2,1)S(1)} %fusion.117), channel_id=1, source_target_pairs={{0,2},{1,3},{2,0},{3,1},{4,6},{5,7},{6,4},{7,5},{8,10},{9,11},{10,... | collective-permute-start | bytes 393224 | tf_op jit(solution)/shard_map/ppermute | solution.py:58
  70.9 6.0 %collective-permute-start.7 = (bf16[128,4,128]{0,1,2:T(4,128)(2,1)S(1)}, bf16[128,4,128]{0,1,2:T(4,128)(2,1)S(1)}, u32[]{:S(2)}, u32[]{:S(2)}) collective-permute-start(bf16[128,4,128]{0,1,2:T(4,128)(2,1)S(1)} %fusion.116), channel_id=1, source_target_pairs={{0,3},{1,0},{2,1},{3,2},{4,7},{5,4},{6,5},{7,6},{8,11},{9,8},{10,9... | collective-permute-start | bytes 393224 | tf_op jit(solution)/shard_map/ppermute | solution.py:58
  82.4 8.8 %collective-permute-start.19 = (bf16[256,4,128]{0,1,2:T(4,128)(2,1)S(1)}, bf16[256,4,128]{0,1,2:T(4,128)(2,1)S(1)}, u32[]{:S(2)}, u32[]{:S(2)}) collective-permute-start(bf16[256,4,128]{0,1,2:T(4,128)(2,1)S(1)} %pad_maximum_fusion.3), channel_id=1, source_target_pairs={{0,2},{1,3},{2,0},{3,1},{4,6},{5,7},{6,4},{7,5},{8,10},{9,11},{10,... | collective-permute-start | bytes 786440 | tf_op jit(solution)/shard_map/ppermute | solution.py:38
  97.3 7.1 %collective-permute-start.23 = (bf16[128,4,1]{0,1,2:T(4,128)(2,1)S(1)}, bf16[128,4,1]{0,1,2:T(4,128)(2,1)S(1)}, u32[]{:S(2)}, u32[]{:S(2)}) collective-permute-start(bf16[128,4,1]{0,1,2:T(4,128)(2,1)S(1)} %get-tuple-element.41), channel_id=1, source_target_pairs={{0,4},{1,5},{2,6},{3,7},{4,8},{5,9},{6,10},{7,11},{8,12},{9,13},{1... | collective-permute-start | bytes 3080 | tf_op jit(solution)/shard_map/ppermute | solution.py:66
  97.6 6.9 %collective-permute-start.24 = (bf16[128,4,1]{0,1,2:T(4,128)(2,1)S(1)}, bf16[128,4,1]{0,1,2:T(4,128)(2,1)S(1)}, u32[]{:S(2)}, u32[]{:S(2)}) collective-permute-start(bf16[128,4,1]{0,1,2:T(4,128)(2,1)S(1)} %get-tuple-element.43), channel_id=1, source_target_pairs={{0,5},{1,6},{2,7},{3,4},{4,9},{5,10},{6,11},{7,8},{8,13},{9,14},{1... | collective-permute-start | bytes 3080 | tf_op jit(solution)/shard_map/ppermute | solution.py:66
  98.4 7.8 %collective-permute-start.25 = (bf16[128,4,1]{0,1,2:T(4,128)(2,1)S(1)}, bf16[128,4,1]{0,1,2:T(4,128)(2,1)S(1)}, u32[]{:S(2)}, u32[]{:S(2)}) collective-permute-start(bf16[128,4,1]{0,1,2:T(4,128)(2,1)S(1)} %get-tuple-element.45), channel_id=1, source_target_pairs={{0,6},{1,7},{2,4},{3,5},{4,10},{5,11},{6,8},{7,9},{8,14},{9,15},{1... | collective-permute-start | bytes 3080 | tf_op jit(solution)/shard_map/ppermute | solution.py:66
  100.1 8.2 %collective-permute-start.26 = (bf16[128,4,1]{0,1,2:T(4,128)(2,1)S(1)}, bf16[128,4,1]{0,1,2:T(4,128)(2,1)S(1)}, u32[]{:S(2)}, u32[]{:S(2)}) collective-permute-start(bf16[128,4,1]{0,1,2:T(4,128)(2,1)S(1)} %get-tuple-element.47), channel_id=1, source_target_pairs={{0,7},{1,4},{2,5},{3,6},{4,11},{5,8},{6,9},{7,10},{8,15},{9,12},{1... | collective-permute-start | bytes 3080 | tf_op jit(solution)/shard_map/ppermute | solution.py:66
  104.4 7.4 %collective-permute-start.20 = (bf16[128,4,128]{0,1,2:T(4,128)(2,1)S(1)}, bf16[128,4,128]{0,1,2:T(4,128)(2,1)S(1)}, u32[]{:S(2)}, u32[]{:S(2)}) collective-permute-start(bf16[128,4,128]{0,1,2:T(4,128)(2,1)S(1)} %fusion.113), channel_id=1, source_target_pairs={{0,1},{1,2},{2,3},{3,0},{4,5},{5,6},{6,7},{7,4},{8,9},{9,10},{10,1... | collective-permute-start | bytes 393224 | tf_op jit(solution)/shard_map/ppermute | solution.py:58
  104.4 5.2 %collective-permute-start.27 = (bf16[128,4,1]{0,1,2:T(4,128)(2,1)S(1)}, bf16[128,4,1]{0,1,2:T(4,128)(2,1)S(1)}, u32[]{:S(2)}, u32[]{:S(2)}) collective-permute-start(bf16[128,4,1]{0,1,2:T(4,128)(2,1)S(1)} %get-tuple-element.42), channel_id=1, source_target_pairs={{0,12},{1,13},{2,14},{3,15},{4,0},{5,1},{6,2},{7,3},{8,4},{9,5},{1... | collective-permute-start | bytes 3080 | tf_op jit(solution)/shard_map/ppermute | solution.py:66
  104.5 6.7 %collective-permute-start.28 = (bf16[128,4,1]{0,1,2:T(4,128)(2,1)S(1)}, bf16[128,4,1]{0,1,2:T(4,128)(2,1)S(1)}, u32[]{:S(2)}, u32[]{:S(2)}) collective-permute-start(bf16[128,4,1]{0,1,2:T(4,128)(2,1)S(1)} %get-tuple-element.44), channel_id=1, source_target_pairs={{0,13},{1,14},{2,15},{3,12},{4,1},{5,2},{6,3},{7,0},{8,5},{9,6},{1... | collective-permute-start | bytes 3080 | tf_op jit(solution)/shard_map/ppermute | solution.py:66
  106.2 5.6 %collective-permute-start.29 = (bf16[128,4,1]{0,1,2:T(4,128)(2,1)S(1)}, bf16[128,4,1]{0,1,2:T(4,128)(2,1)S(1)}, u32[]{:S(2)}, u32[]{:S(2)}) collective-permute-start(bf16[128,4,1]{0,1,2:T(4,128)(2,1)S(1)} %get-tuple-element.46), channel_id=1, source_target_pairs={{0,14},{1,15},{2,12},{3,13},{4,2},{5,3},{6,0},{7,1},{8,6},{9,7},{1... | collective-permute-start | bytes 3080 | tf_op jit(solution)/shard_map/ppermute | solution.py:66
  109.6 6.3 %collective-permute-start.21 = (bf16[128,4,128]{0,1,2:T(4,128)(2,1)S(1)}, bf16[128,4,128]{0,1,2:T(4,128)(2,1)S(1)}, u32[]{:S(2)}, u32[]{:S(2)}) collective-permute-start(bf16[128,4,128]{0,1,2:T(4,128)(2,1)S(1)} %fusion.112), channel_id=1, source_target_pairs={{0,2},{1,3},{2,0},{3,1},{4,6},{5,7},{6,4},{7,5},{8,10},{9,11},{10,... | collective-permute-start | bytes 393224 | tf_op jit(solution)/shard_map/ppermute | solution.py:58
  111.3 4.6 %collective-permute-start.22 = (bf16[128,4,128]{0,1,2:T(4,128)(2,1)S(1)}, bf16[128,4,128]{0,1,2:T(4,128)(2,1)S(1)}, u32[]{:S(2)}, u32[]{:S(2)}) collective-permute-start(bf16[128,4,128]{0,1,2:T(4,128)(2,1)S(1)} %fusion.111), channel_id=1, source_target_pairs={{0,3},{1,0},{2,1},{3,2},{4,7},{5,4},{6,5},{7,6},{8,11},{9,8},{10,9... | collective-permute-start | bytes 393224 | tf_op jit(solution)/shard_map/ppermute | solution.py:58
  120.7 8.4 %collective-permute-start.32 = (bf16[256,4,128]{0,1,2:T(4,128)(2,1)S(1)}, bf16[256,4,128]{0,1,2:T(4,128)(2,1)S(1)}, u32[]{:S(2)}, u32[]{:S(2)}) collective-permute-start(bf16[256,4,128]{0,1,2:T(4,128)(2,1)S(1)} %pad_maximum_fusion.4), channel_id=1, source_target_pairs={{0,2},{1,3},{2,0},{3,1},{4,6},{5,7},{6,4},{7,5},{8,10},{9,11},{10,... | collective-permute-start | bytes 786440 | tf_op jit(solution)/shard_map/ppermute | solution.py:38
  135.8 5.9 %collective-permute-start.34 = (bf16[128,4,128]{0,1,2:T(4,128)(2,1)S(1)}, bf16[128,4,128]{0,1,2:T(4,128)(2,1)S(1)}, u32[]{:S(2)}, u32[]{:S(2)}) collective-permute-start(bf16[128,4,128]{0,1,2:T(4,128)(2,1)S(1)} %fusion.107), channel_id=1, source_target_pairs={{0,2},{1,3},{2,0},{3,1},{4,6},{5,7},{6,4},{7,5},{8,10},{9,11},{10,... | collective-permute-start | bytes 393224 | tf_op jit(solution)/shard_map/ppermute | solution.py:58
  137.5 5.7 %collective-permute-start.35 = (bf16[128,4,128]{0,1,2:T(4,128)(2,1)S(1)}, bf16[128,4,128]{0,1,2:T(4,128)(2,1)S(1)}, u32[]{:S(2)}, u32[]{:S(2)}) collective-permute-start(bf16[128,4,128]{0,1,2:T(4,128)(2,1)S(1)} %fusion.106), channel_id=1, source_target_pairs={{0,3},{1,0},{2,1},{3,2},{4,7},{5,4},{6,5},{7,6},{8,11},{9,8},{10,9... | collective-permute-start | bytes 393224 | tf_op jit(solution)/shard_map/ppermute | solution.py:58
  (8 other events, 84.6 us)
